TPU v7x, 128 devices: a whole 4x4x4 slice. The times are simulated.
128 devices in a mesh: fsdp: 8 (over x, z_lo), dp: 16 (over z_hi, y, core).
Axes of the slice: x: 4, y: 4, z: 4 (z_hi: 2, z_lo: 2; z = z_hi * 2 + z_lo), core: 2. Of those that a mesh axis runs over, the one named last changes fastest.
Arguments:
- tokens: bfloat16 [8, 2176, 3200], P('fsdp', 'dp'), may hold values from -6 to 6
- norm_gain: float32 [3200], replicated, may hold values from 0.5 to 1.5
- qkv_weight: bfloat16 [3200, 6144], P('fsdp', 'dp'), may hold values from -4 to 4
- qk_gain: float32 [2, 2048], P(None, 'dp'), may hold values from 1 to 8
- out_weight: bfloat16 [2048, 3200], P('dp', 'fsdp'), may hold values from -0.125 to 0.125
- layer_scale: float32 [3200], replicated, may hold values from 0.2 to 1
- tile_counts: int32 [8, 2], replicated, may hold values from 0 to 2, as said below
- owners: int32 [8, 2], replicated, may hold values from 0 to 7, as said below
Outputs:
- vision_tokens: bfloat16 [32, 256, 12800], P('fsdp', None, 'dp')
Inputs may be any that keep to these rules, and one draw needn't show every extreme that they name: `tile_counts`: column 0 is 1 to 2, column 1 is 0 to 2 minus column 0. All owners together get at most 4 live tiles each, and one owner gets exactly 4.
All inputs are finite; a program needn't handle non-finite values.
Results may differ from a plain program's by a relative error of at most 0.006.
The roundings to bfloat16 on the way count: a program that leaves them out, or rounds other values in their place, can miss the bound.
Values may be sent and summed in bfloat16 or wider, within the bound.
No kernel may reach another device: no remote copies, remote signals or barrier semaphores. Data moves between devices by JAX's collectives and lax.ppermute only.
A program may use at most 192 MiB of HBM per device.

v0:
```python
import jax
import jax.numpy as jnp
from jax import lax
from jax.sharding import PartitionSpec as P

HEAD_DIM = 128
GRID = 32
SLOTS = 2
TILE = 1025
CAP = 4
EPSILON = 1e-06


def merge_tiles(values):
    halves = GRID // 2
    columns = values.shape[1]
    tile_list = []
    for tile_slot in range(SLOTS):
        patches = values[tile_slot * TILE + 1 : (tile_slot + 1) * TILE]
        square = patches.reshape(halves, 2, halves, 2, columns).transpose(0, 2, 4, 1, 3)
        tile_list.append(square.reshape(halves * halves, columns * 4))
    return jnp.stack(tile_list)


def tile_owners(tile_counts, owners):
    slot_index = jnp.arange(SLOTS, dtype=jnp.int32)[None, :]
    first_count = tile_counts[:, 0:1]
    holder = jnp.where(slot_index < first_count, owners[:, 0:1], owners[:, 1:2])
    living = slot_index < first_count + tile_counts[:, 1:2]
    return (holder, living)


def place_tiles(received, holder, living, target):
    owned_flag = jnp.logical_and(living, holder == target).reshape(-1).astype(jnp.int32)
    before = jnp.cumsum(owned_flag) - owned_flag
    chosen = jnp.logical_and(
        before[None, :] == jnp.arange(CAP, dtype=jnp.int32)[:, None], owned_flag[None, :] == 1
    )
    flattened = received.reshape(received.shape[0] * received.shape[1], -1)
    placed = jnp.dot(chosen.astype(jnp.bfloat16), flattened, preferred_element_type=jnp.float32)
    return placed.astype(jnp.bfloat16).reshape(CAP, received.shape[2], received.shape[3])


def body(tokens, norm_gain, qkv_weight, qk_gain, out_weight, layer_scale, tile_counts, owners):
    own_rows = tokens[0]
    gathered = lax.all_gather(own_rows, "dp", axis=0, tiled=True)
    length = gathered.shape[0]
    model_width = gathered.shape[1]
    groups = lax.axis_size("dp")
    values = gathered.astype(jnp.float32)
    normed = (
        values * lax.rsqrt(jnp.mean(values * values, axis=-1, keepdims=True) + EPSILON) * norm_gain
    ).astype(jnp.bfloat16)
    projected = jnp.dot(
        normed,
        lax.all_gather(qkv_weight, "fsdp", axis=0, tiled=True),
        preferred_element_type=jnp.float32,
    )
    queries = projected[:, :HEAD_DIM]
    keys_part = projected[:, HEAD_DIM : 2 * HEAD_DIM]
    values_part = projected[:, 2 * HEAD_DIM :].astype(jnp.bfloat16)
    query_sums, key_sums = lax.psum(
        (jnp.sum(queries * queries, axis=-1), jnp.sum(keys_part * keys_part, axis=-1)), "dp"
    )
    window = groups * HEAD_DIM
    queries = (queries * lax.rsqrt(query_sums / window + EPSILON)[:, None] * qk_gain[0]).astype(
        jnp.bfloat16
    )
    keys_part = (keys_part * lax.rsqrt(key_sums / window + EPSILON)[:, None] * qk_gain[1]).astype(
        jnp.bfloat16
    )
    row_index = lax.axis_index("fsdp")
    row_count = lax.axis_size("fsdp")
    factor = HEAD_DIM ** (-0.5)
    covered = SLOTS * TILE
    tile_query = queries[:covered].reshape(SLOTS, TILE, HEAD_DIM)
    tile_key = keys_part[:covered].reshape(SLOTS, TILE, HEAD_DIM)
    tile_value = values_part[:covered].reshape(SLOTS, TILE, HEAD_DIM)
    scores = (
        jnp.einsum("sqc,skc->sqk", tile_query, tile_key, preferred_element_type=jnp.float32)
        * factor
    )
    highest = jnp.max(scores, axis=-1, keepdims=True)
    exponent = jnp.exp(scores - highest)
    weights = (exponent / jnp.sum(exponent, axis=-1, keepdims=True)).astype(jnp.bfloat16)
    tile_out = jnp.einsum(
        "sqk,skc->sqc", weights, tile_value, preferred_element_type=jnp.float32
    ).astype(jnp.bfloat16)
    head_out = jnp.concatenate(
        [
            tile_out.reshape(covered, HEAD_DIM),
            jnp.zeros((length - covered, HEAD_DIM), jnp.bfloat16),
        ],
        axis=0,
    )
    dp_index = lax.axis_index("dp")
    block = model_width // groups
    head_rows = lax.all_gather(out_weight, "fsdp", axis=1, tiled=True)
    weight_block = lax.all_to_all(head_rows, "dp", split_axis=1, concat_axis=0, tiled=True)
    all_heads = lax.all_gather(head_out, "dp", axis=0, tiled=False)
    head_terms = jnp.einsum(
        "hsc,hcd->hsd",
        all_heads,
        weight_block.reshape(groups, HEAD_DIM, block),
        preferred_element_type=jnp.float32,
    ).astype(jnp.bfloat16)
    attention = jnp.sum(lax.optimization_barrier(head_terms).astype(jnp.float32), axis=0)
    own_block = lax.dynamic_slice_in_dim(gathered, dp_index * block, block, axis=1)
    scale_block = lax.dynamic_slice_in_dim(layer_scale, dp_index * block, block)
    updated = (own_block.astype(jnp.float32) + scale_block * attention).astype(jnp.bfloat16)
    merged = merge_tiles(updated)
    holder, living = tile_owners(tile_counts, owners)
    own_holder = holder[row_index]
    own_living = living[row_index]
    destination = jnp.arange(row_count, dtype=jnp.int32)[:, None]
    sending = jnp.logical_and(destination == own_holder[None, :], own_living[None, :])
    outgoing = jnp.where(sending[:, :, None, None], merged[None], jnp.zeros((), jnp.bfloat16))
    received = lax.all_to_all(outgoing, "fsdp", split_axis=0, concat_axis=0, tiled=True)
    return place_tiles(received, holder, living, row_index)


def solution(mesh):
    placed = (
        P("fsdp", "dp", None),
        P(),
        P("fsdp", "dp"),
        P(None, "dp"),
        P("dp", "fsdp"),
        P(),
        P(),
        P(),
    )
    return jax.shard_map(
        body, mesh=mesh, in_specs=placed, out_specs=P("fsdp", None, "dp"), check_vma=False
    )
```

profile of v0, /device:TPU:1, one launch (start us, length us, event | category | flops | bytes accessed | tf_op | source)
XLA Modules:
  0.0 529.9 jit_solution(8321030742287554255)
XLA Ops:
  6.5 0.0 all-gather.8.cloned.1.call-start
  6.5 0.7 all-gather.8.cloned.1.call-update
  7.3 0.0 all-gather.6.cloned.1.call-start
  7.3 0.7 all-gather.6.cloned.1.call-update
  8.0 0.0 all-gather.10.cloned.1.call-start
  8.1 0.8 slice_bitcast_fusion
  8.8 101.3 %all-gather.8.cloned.1.call-done = bf16[1,2176,3200]{2,1,0:T(8,128)(2,1)} async-done(((bf16[1,136,3200]{2,1,0:T(8,128)(2,1)}), bf16[1,2176,3200]{2,1,0:T(8,128)(2,1)}) %all-gather.8.cloned.1.call-update) | async-done | bytes 13926416 | tf_op jit(solution)/shard_map/all_gather | solution.py:46
  110.2 7.7 %fusion.1 = f32[2176]{0:T(1024)S(1)} fusion(bf16[1,2176,3200]{2,1,0:T(8,128)(2,1)} %all-gather.8.cloned.1.call-done), kind=kLoop, calls=%fused_computation.4 | loop fusion | flops 20887424 | bytes 13935104 | tf_op jit(solution)/shard_map/reduce_sum | solution.py:52
  117.9 47.7 %all-gather.6.cloned.1.call-done = bf16[3200,384]{1,0:T(8,128)(2,1)} async-done(((bf16[400,384]{1,0:T(8,128)(2,1)}), bf16[3200,384]{1,0:T(8,128)(2,1)}) %all-gather.6.cloned.1.call-update) | async-done | bytes 2457616 | tf_op jit(solution)/shard_map/all_gather | solution.py:56
  165.6 0.0 copy-done.4
  165.6 11.8 %fusion.5 = f32[2176,384]{1,0:T(8,128)S(1)} fusion(bf16[3200,384]{1,0:T(8,128)(2,1)} %all-gather.6.cloned.1.call-done, bf16[1,2176,3200]{2,1,0:T(8,128)(2,1)} %all-gather.8.cloned.1.call-done, f32[3200]{0:T(1024)S(1)} %copy-done.4, f32[2176]{0:T(1024)S(1)} %add_rsqrt_fusion.2), kind=kOutput, calls=%fused_computation.11 | convolution fusion | flops 5375590400 | bytes 19747840 | tf_op jit(solution)/shard_map/dot_general | solution.py:54
  177.5 0.1 slice.84
  177.5 0.6 multiply_reduce_fusion
  178.2 65.0 %all-reduce.1 = (f32[2176]{0:T(1024)S(1)}, f32[2176]{0:T(1024)S(1)}) all-reduce(f32[2176]{0:T(1024)S(1)} %get-tuple-element.6, f32[2176]{0:T(1024)S(1)} %get-tuple-element.5), channel_id=1, replica_groups=mesh['fsdp'=8,'dp'=16] {'dp'}, use_global_device_ids=true, to_apply=%region_3.0 | all-reduce | flops 4352 | bytes 34816 | tf_op jit(solution)/shard_map/psum | solution.py:62
  243.2 0.9 reshape.243
  244.1 1.1 fusion.15
  245.2 0.1 reshape.242
  245.3 0.0 copy-start
  245.3 0.1 reshape.241
  245.5 3.2 fusion.32
  248.7 0.0 copy-done
  248.7 0.0 copy-start.1
  248.7 0.0 copy-start.2
  248.7 0.0 copy-start.3
  248.7 4.9 fusion.12
  253.6 0.1 reshape.244
  253.7 0.8 concatenate.3
  254.6 0.0 all-gather.10.cloned.1.call-update
  254.6 0.0 copy-done.1
  254.6 27.5 %all_gather.19 = bf16[128,3200]{0,1:T(8,128)(2,1)} all-gather(bf16[128,400]{0,1:T(8,128)(2,1)S(1)} %copy-done.1), channel_id=1, replica_groups=mesh['fsdp'=8,'dp'=16] {'fsdp'}, dimensions={1}, use_global_device_ids=true | all-gather | bytes 921600 | tf_op jit(solution)/shard_map/all_gather | solution.py:98
  282.1 15.1 %all-to-all-start = ((bf16[128,16,200]{0,2,1:T(8,128)(2,1)}), bf16[128,16,200]{0,2,1:T(8,128)(2,1)S(1)}, u32[]{:S(2)}, u32[]{:S(2)}) async-start(bf16[128,16,200]{0,2,1:T(8,128)(2,1)} %bitcast.12), calls=%async_computation | async-start | bytes 1638400 | tf_op jit(solution)/shard_map/all_to_all | solution.py:99
  297.2 0.0 copy-done.2
  297.2 0.1 fusion.19
  297.3 0.1 and_convert_fusion
  297.4 0.8 dynamic_slice.15
  298.2 2.5 constant_dynamic-slice_fusion
  300.7 0.8 copy.37
  301.5 14.2 %all-to-all-done = bf16[128,16,200]{0,2,1:T(8,128)(2,1)S(1)} async-done(((bf16[128,16,200]{0,2,1:T(8,128)(2,1)}), bf16[128,16,200]{0,2,1:T(8,128)(2,1)S(1)}, u32[]{:S(2)}, u32[]{:S(2)}) %all-to-all-start) | async-done | bytes 819232 | tf_op jit(solution)/shard_map/all_to_all | solution.py:99
  315.7 31.7 %all-gather.10.cloned.1.call-done = bf16[34816,128]{1,0:T(8,128)(2,1)} async-done(((bf16[2176,128]{1,0:T(8,128)(2,1)}), bf16[34816,128]{1,0:T(8,128)(2,1)}) %all-gather.10.cloned.1.call-update) | async-done | bytes 8912912 | tf_op jit(solution)/shard_map/all_gather | solution.py:100
  347.3 10.8 %convolution_convert_fusion.1 = bf16[16,2176,200]{1,2,0:T(8,128)(2,1)} fusion(bf16[16,2176,128]{2,1,0:T(8,128)(2,1)} %bitcast.53, bf16[128,16,200]{0,2,1:T(8,128)(2,1)S(1)} %all-to-all-done), kind=kOutput, calls=%fused_computation.8 | convolution fusion | flops 1789542400 | bytes 23658496 | tf_op jit(solution)/shard_map/hsc,hcd->hsd/dot_general | solution.py:101
  358.2 7.3 %convert_reduce_fusion = f32[2176,200]{0,1:T(8,128)S(1)} fusion(bf16[16,2176,200]{1,2,0:T(8,128)(2,1)} %convolution_convert_fusion.1), kind=kLoop, calls=%fused_computation.7 | loop fusion | flops 13491200 | bytes 15667200 | tf_op jit(solution)/shard_map/reduce_sum | solution.py:107
  365.5 0.3 fusion.13
  365.8 0.4 fusion.31
  366.1 0.2 copy.30
  366.4 1.0 reshape.245
  367.4 0.2 copy.32
  367.6 1.1 reshape.246
  368.7 4.9 copy.33
  373.5 3.9 stack_reshape.7
  377.4 4.9 copy.31
  382.3 3.8 stack_reshape.6
  386.1 1.2 pad_maximum_fusion
  387.3 3.3 broadcast_select_fusion
  390.7 5.0 all-to-all-start.1
  395.6 0.1 reshape.250
  395.7 0.1 reshape.256
  395.8 0.1 reduce
  396.0 90.6 %all-to-all-done.1 = bf16[8,2,256,800]{2,3,1,0:T(8,128)(2,1)} async-done(((bf16[8,2,256,800]{2,3,1,0:T(8,128)(2,1)}), bf16[8,2,256,800]{2,3,1,0:T(8,128)(2,1)}, u32[]{:S(2)}, u32[]{:S(2)}) %all-to-all-start.1) | async-done | bytes 6553632 | tf_op jit(solution)/shard_map/all_to_all | solution.py:118
  486.6 11.1 %copy.34 = bf16[8,2,256,800]{3,2,1,0:T(8,128)(2,1)} copy(bf16[8,2,256,800]{2,3,1,0:T(8,128)(2,1)} %all-to-all-done.1) | data formatting | bytes 13107200 | tf_op jit(solution)/shard_map/all_to_all | solution.py:118
  497.7 14.7 %reshape.247 = bf16[16,204800]{1,0:T(8,128)(2,1)} reshape(bf16[8,2,256,800]{3,2,1,0:T(8,128)(2,1)} %copy.34) | data formatting | bytes 13107200 | tf_op jit(solution)/shard_map/reshape | solution.py:39
  512.4 4.0 convolution_convert_fusion
  516.4 1.6 reshape.258
  518.0 2.8 reshape.248
  520.8 2.3 copy.35
  (12 shorter events, 0.1 us)
Async XLA Ops:
  6.5 103.6 %all-gather.8.cloned.1.call-start = ((), (), s32[]{:S(2)}) async-start(), calls=%async_computation.3 | async-start | bytes 14796800 | tf_op jit(solution)/shard_map/all_gather | solution.py:46
  7.3 158.4 %all-gather.6.cloned.1.call-start = ((), (), s32[]{:S(2)}) async-start(), calls=%async_computation.2 | async-start | bytes 2764800 | tf_op jit(solution)/shard_map/all_gather | solution.py:56
  8.0 339.3 %all-gather.10.cloned.1.call-start = ((), (), s32[]{:S(2)}) async-start(), calls=%async_computation.4 | async-start | bytes 9469952 | tf_op jit(solution)/shard_map/all_gather | solution.py:100
  8.8 156.8 %copy-start.4 = (f32[3200]{0:T(1024)S(1)}, f32[3200]{0:T(1024)}, u32[]{:S(2)}) copy-start(f32[3200]{0:T(1024)} %param.9) | copy-start | bytes 38404
  245.3 3.4 copy-start
  248.7 5.9 %copy-start.1 = (bf16[128,400]{0,1:T(8,128)(2,1)S(1)}, bf16[128,400]{0,1:T(8,128)(2,1)}, u32[]{:S(2)}) copy-start(bf16[128,400]{0,1:T(8,128)(2,1)} %param.12) | copy-start | bytes 307204
  248.7 48.5 %copy-start.2 = (s32[8,2]{0,1:T(2,128)S(1)}, s32[8,2]{0,1:T(2,128)}, u32[]{:S(2)}) copy-start(s32[8,2]{0,1:T(2,128)} %param.15) | copy-start | bytes 196
  248.7 48.5 %copy-start.3 = (s32[8,2]{0,1:T(2,128)S(1)}, s32[8,2]{0,1:T(2,128)}, u32[]{:S(2)}) copy-start(s32[8,2]{0,1:T(2,128)} %param.14) | copy-start | bytes 196
  282.1 33.6 %all-to-all-start = ((bf16[128,16,200]{0,2,1:T(8,128)(2,1)}), bf16[128,16,200]{0,2,1:T(8,128)(2,1)S(1)}, u32[]{:S(2)}, u32[]{:S(2)}) async-start(bf16[128,16,200]{0,2,1:T(8,128)(2,1)} %bitcast.12), calls=%async_computation | async-start | bytes 1638400 | tf_op jit(solution)/shard_map/all_to_all | solution.py:99
  390.7 95.9 %all-to-all-start.1 = ((bf16[8,2,256,800]{2,3,1,0:T(8,128)(2,1)}), bf16[8,2,256,800]{2,3,1,0:T(8,128)(2,1)}, u32[]{:S(2)}, u32[]{:S(2)}) async-start(bf16[8,2,256,800]{2,3,1,0:T(8,128)(2,1)} %broadcast_select_fusion), calls=%async_computation.1 | async-start | bytes 13107200 | tf_op jit(solution)/shard_map/all_to_all | solution.py:118
Sparse Core Ops, SparseCore 0:
  9.8 100.3 all-gather.7
  111.8 53.8 all-gather.5
  254.7 92.5 all-gather.9
where the time goes:
time: 535 us; the launch traced here: 530 us
  waiting for transfers between devices  287 us (54%)
  blocking collectives  92.5 us (17%)
  local copies, waits for them, and re-layouts  59.9 us (11%)
  matrix products  34.7 us (6%)
  other arithmetic  22 us (4%)
  starting transfers between devices  20.1 us (4%)
  between operations  13.6 us (3%)
    all_gather x1, waiting for transfers between devices, body(): gathered = lax.all_gather(own_rows, 'dp', axis=0, tiled=True)  101 us
    all_to_all x1, waiting for transfers between devices, body(): lax.all_to_all(outgoing, 'fsdp', split_axis=0, concat_axis=0, tiled=True)  90.6 us
    psum x1, blocking collectives, body(): lax.psum((jnp.sum(queries * queries, axis=-1), jnp.sum(keys_part * keys_p...  65 us
    all_gather x1, waiting for transfers between devices, body(): lax.all_gather(qkv_weight, 'fsdp', axis=0, tiled=True)  47.7 us
    all_gather x1, waiting for transfers between devices, body(): all_heads = lax.all_gather(head_out, 'dp', axis=0, tiled=False)  31.7 us
    all_gather x1, blocking collectives, body(): head_rows = lax.all_gather(out_weight, 'fsdp', axis=1, tiled=True)  27.5 us
    all_to_all x1, starting transfers between devices, body(): lax.all_to_all(head_rows, 'dp', split_axis=1, concat_axis=0, tiled=True)  15.1 us
    reshape x1, local copies, waits for them, and re-layouts, place_tiles(): flattened = received.reshape(received.shape[0] * received.shape[1], -1)  14.7 us
  transfers between devices with their start and end apart: 5, of which 5 were waited for; matrix products, arithmetic and copies ran while one was open for 2% of the time, Pallas kernels for 0%

commit v1 on v0

--- a/solution.py
+++ b/solution.py
@@ -53,7 +53,9 @@
     ).astype(jnp.bfloat16)
     projected = jnp.dot(
         normed,
-        lax.all_gather(qkv_weight, "fsdp", axis=0, tiled=True),
+        jnp.concatenate(
+            lax.all_to_all(jnp.stack([qkv_weight] * lax.axis_size("fsdp")), "fsdp", 0, 0), axis=0
+        ),
         preferred_element_type=jnp.float32,
     )
     queries = projected[:, :HEAD_DIM]

time: 535 us -> 503 us (0.940)
  waiting for transfers between devices: 287 us -> 251 us
    all_gather x1 -> x0, waiting for transfers between devices: 47.7 us -> none  [body(): lax.all_gather(qkv_weight, 'fsdp', axis=0, tiled=True)]
    all_gather x1, waiting for transfers between devices: 101 us -> 114 us  [body(): gathered = lax.all_gather(own_rows, 'dp', axis=0, tiled=True)]
    all_to_all x0 -> x1, starting transfers between devices: none -> 6.19 us  [body(): lax.all_to_all(jnp.stack([qkv_weight] * lax.axis_size('fsdp')), 'fsdp', 0...]
  transfers between devices with their start and end apart: 5 -> 5, of which waited for: 5 -> 4; matrix products, arithmetic and copies ran while one was open for 2% -> 3% of each run, Pallas kernels for 0% -> 0%
where the time goes in v1:
time: 503 us; the launch traced here: 497 us
  waiting for transfers between devices  251 us (50%)
  blocking collectives  90.1 us (18%)
  local copies, waits for them, and re-layouts  61.8 us (12%)
  matrix products  33.9 us (7%)
  starting transfers between devices  24.8 us (5%)
  other arithmetic  22 us (4%)
  between operations  13.9 us (3%)
    all_gather x1, waiting for transfers between devices, body(): gathered = lax.all_gather(own_rows, 'dp', axis=0, tiled=True)  114 us
    all_to_all x1, waiting for transfers between devices, body(): lax.all_to_all(outgoing, 'fsdp', split_axis=0, concat_axis=0, tiled=True)  90.6 us
    psum x1, blocking collectives, body(): lax.psum((jnp.sum(queries * queries, axis=-1), jnp.sum(keys_part * keys_p...  60.2 us
    all_gather x1, waiting for transfers between devices, body(): all_heads = lax.all_gather(head_out, 'dp', axis=0, tiled=False)  31.6 us
    all_gather x1, blocking collectives, body(): head_rows = lax.all_gather(out_weight, 'fsdp', axis=1, tiled=True)  29.9 us
    reshape x1, local copies, waits for them, and re-layouts, place_tiles(): flattened = received.reshape(received.shape[0] * received.shape[1], -1)  14.7 us
    all_to_all x1, waiting for transfers between devices, body(): lax.all_to_all(head_rows, 'dp', split_axis=1, concat_axis=0, tiled=True)  14.2 us
    all_to_all x1, starting transfers between devices, body(): lax.all_to_all(head_rows, 'dp', split_axis=1, concat_axis=0, tiled=True)  13.6 us
  transfers between devices with their start and end apart: 5, of which 4 were waited for; matrix products, arithmetic and copies ran while one was open for 3% of the time, Pallas kernels for 0%

profile of v1, /device:TPU:1, one launch (start us, length us, event | category | flops | bytes accessed | tf_op | source)
XLA Modules:
  0.0 497.1 jit_solution(13555578694489103789)
XLA Ops:
  6.5 0.0 all-gather.5.cloned.1.call-start
  6.5 0.7 all-gather.5.cloned.1.call-update
  7.3 2.6 stack.4
  9.9 6.2 %all-to-all-start = ((bf16[8,400,384]{2,1,0:T(8,128)(2,1)}), bf16[8,400,384]{2,1,0:T(8,128)(2,1)S(1)}, u32[]{:S(2)}, u32[]{:S(2)}) async-start(bf16[8,400,384]{2,1,0:T(8,128)(2,1)} %stack.4), calls=%async_computation | async-start | bytes 4915200 | tf_op jit(solution)/shard_map/all_to_all | solution.py:57
  16.0 0.0 all-gather.7.cloned.1.call-start
  16.1 0.0 copy-done.2
  16.1 0.0 copy-start.5
  16.1 113.5 %all-gather.5.cloned.1.call-done = bf16[1,2176,3200]{2,1,0:T(8,128)(2,1)} async-done(((bf16[1,136,3200]{2,1,0:T(8,128)(2,1)}), bf16[1,2176,3200]{2,1,0:T(8,128)(2,1)}) %all-gather.5.cloned.1.call-update) | async-done | bytes 13926416 | tf_op jit(solution)/shard_map/all_gather | solution.py:46
  129.7 7.7 %fusion.1 = f32[2176]{0:T(1024)S(1)} fusion(bf16[1,2176,3200]{2,1,0:T(8,128)(2,1)} %all-gather.5.cloned.1.call-done), kind=kLoop, calls=%fused_computation.4 | loop fusion | flops 20887424 | bytes 13935104 | tf_op jit(solution)/shard_map/reduce_sum | solution.py:52
  137.4 0.0 all-to-all-done
  137.4 11.0 %fusion.5 = f32[2176,384]{1,0:T(8,128)S(1)} fusion(bf16[3200,384]{1,0:T(8,128)(2,1)S(1)} %bitcast.55, bf16[1,2176,3200]{2,1,0:T(8,128)(2,1)} %all-gather.5.cloned.1.call-done, f32[3200]{0:T(1024)S(1)} %copy-done.5, f32[2176]{0:T(1024)S(1)} %add_rsqrt_fusion.2), kind=kOutput, calls=%fused_computation.11 | convolution fusion | flops 5375590400 | bytes 19747840 | tf_op jit(solution)/shard_map/dot_general | solution.py:54
  148.5 0.1 slice.84
  148.5 0.6 multiply_reduce_fusion
  149.2 60.2 %all-reduce.1 = (f32[2176]{0:T(1024)S(1)}, f32[2176]{0:T(1024)S(1)}) all-reduce(f32[2176]{0:T(1024)S(1)} %get-tuple-element.6, f32[2176]{0:T(1024)S(1)} %get-tuple-element.5), channel_id=1, replica_groups=mesh['fsdp'=8,'dp'=16] {'dp'}, use_global_device_ids=true, to_apply=%region_3.0 | all-reduce | flops 4352 | bytes 34816 | tf_op jit(solution)/shard_map/psum | solution.py:64
  209.4 0.9 reshape.249
  210.3 1.1 fusion.15
  211.4 0.1 reshape.248
  211.5 0.0 copy-start
  211.5 0.1 reshape.247
  211.7 3.2 fusion.32
  214.9 0.0 copy-start.1
  214.9 0.0 copy-start.3
  214.9 0.0 copy-start.4
  214.9 4.9 fusion.12
  219.8 0.1 reshape.250
  219.9 0.8 concatenate.3
  220.7 0.0 all-gather.7.cloned.1.call-update
  220.8 0.0 copy-done.1
  220.8 29.9 %all_gather.15 = bf16[128,3200]{0,1:T(8,128)(2,1)} all-gather(bf16[128,400]{0,1:T(8,128)(2,1)S(1)} %copy-done.1), channel_id=1, replica_groups=mesh['fsdp'=8,'dp'=16] {'fsdp'}, dimensions={1}, use_global_device_ids=true | all-gather | bytes 921600 | tf_op jit(solution)/shard_map/all_gather | solution.py:100
  250.7 13.6 %all-to-all-start.1 = ((bf16[128,16,200]{0,2,1:T(8,128)(2,1)}), bf16[128,16,200]{0,2,1:T(8,128)(2,1)S(1)}, u32[]{:S(2)}, u32[]{:S(2)}) async-start(bf16[128,16,200]{0,2,1:T(8,128)(2,1)} %bitcast.13), calls=%async_computation.1 | async-start | bytes 1638400 | tf_op jit(solution)/shard_map/all_to_all | solution.py:101
  264.2 0.0 copy-done.3
  264.3 0.0 copy-done.4
  264.3 0.1 fusion.19
  264.4 0.1 and_convert_fusion
  264.4 0.8 dynamic_slice.15
  265.2 2.5 constant_dynamic-slice_fusion
  267.7 0.8 copy.37
  268.5 14.2 %all-to-all-done.1 = bf16[128,16,200]{0,2,1:T(8,128)(2,1)S(1)} async-done(((bf16[128,16,200]{0,2,1:T(8,128)(2,1)}), bf16[128,16,200]{0,2,1:T(8,128)(2,1)S(1)}, u32[]{:S(2)}, u32[]{:S(2)}) %all-to-all-start.1) | async-done | bytes 819232 | tf_op jit(solution)/shard_map/all_to_all | solution.py:101
  282.7 31.6 %all-gather.7.cloned.1.call-done = bf16[34816,128]{1,0:T(8,128)(2,1)} async-done(((bf16[2176,128]{1,0:T(8,128)(2,1)}), bf16[34816,128]{1,0:T(8,128)(2,1)}) %all-gather.7.cloned.1.call-update) | async-done | bytes 8912912 | tf_op jit(solution)/shard_map/all_gather | solution.py:102
  314.3 10.8 %convolution_convert_fusion.1 = bf16[16,2176,200]{1,2,0:T(8,128)(2,1)} fusion(bf16[16,2176,128]{2,1,0:T(8,128)(2,1)} %bitcast.54, bf16[128,16,200]{0,2,1:T(8,128)(2,1)S(1)} %all-to-all-done.1), kind=kOutput, calls=%fused_computation.8 | convolution fusion | flops 1789542400 | bytes 23658496 | tf_op jit(solution)/shard_map/hsc,hcd->hsd/dot_general | solution.py:103
  325.1 7.3 %convert_reduce_fusion = f32[2176,200]{0,1:T(8,128)S(1)} fusion(bf16[16,2176,200]{1,2,0:T(8,128)(2,1)} %convolution_convert_fusion.1), kind=kLoop, calls=%fused_computation.7 | loop fusion | flops 13491200 | bytes 15667200 | tf_op jit(solution)/shard_map/reduce_sum | solution.py:109
  332.5 0.3 fusion.13
  332.7 0.4 fusion.31
  333.1 0.2 copy.30
  333.3 1.0 reshape.251
  334.4 0.2 copy.32
  334.6 1.1 reshape.252
  335.6 4.9 copy.33
  340.5 3.9 stack_reshape.7
  344.4 4.9 copy.31
  349.2 3.8 stack_reshape.6
  353.1 1.2 pad_maximum_fusion
  354.3 3.3 broadcast_select_fusion
  357.6 5.0 %all-to-all-start.2 = ((bf16[8,2,256,800]{2,3,1,0:T(8,128)(2,1)}), bf16[8,2,256,800]{2,3,1,0:T(8,128)(2,1)}, u32[]{:S(2)}, u32[]{:S(2)}) async-start(bf16[8,2,256,800]{2,3,1,0:T(8,128)(2,1)} %broadcast_select_fusion), calls=%async_computation.2 | async-start | bytes 13107200 | tf_op jit(solution)/shard_map/all_to_all | solution.py:120
  362.6 0.1 reshape.256
  362.7 0.1 reshape.262
  362.8 0.1 reduce
  362.9 90.6 %all-to-all-done.2 = bf16[8,2,256,800]{2,3,1,0:T(8,128)(2,1)} async-done(((bf16[8,2,256,800]{2,3,1,0:T(8,128)(2,1)}), bf16[8,2,256,800]{2,3,1,0:T(8,128)(2,1)}, u32[]{:S(2)}, u32[]{:S(2)}) %all-to-all-start.2) | async-done | bytes 6553632 | tf_op jit(solution)/shard_map/all_to_all | solution.py:120
  453.6 11.1 %copy.34 = bf16[8,2,256,800]{3,2,1,0:T(8,128)(2,1)} copy(bf16[8,2,256,800]{2,3,1,0:T(8,128)(2,1)} %all-to-all-done.2) | data formatting | bytes 13107200 | tf_op jit(solution)/shard_map/all_to_all | solution.py:120
  464.6 14.7 %reshape.253 = bf16[16,204800]{1,0:T(8,128)(2,1)} reshape(bf16[8,2,256,800]{3,2,1,0:T(8,128)(2,1)} %copy.34) | data formatting | bytes 13107200 | tf_op jit(solution)/shard_map/reshape | solution.py:39
  479.4 4.0 convolution_convert_fusion
  483.3 1.6 reshape.264
  485.0 2.8 reshape.254
  487.7 2.3 copy.35
  (14 shorter events, 0.1 us)
Async XLA Ops:
  6.5 9.6 %copy-start.2 = (f32[2,128]{1,0:T(2,128)S(1)}, f32[2,128]{1,0:T(2,128)}, u32[]{:S(2)}) copy-start(f32[2,128]{1,0:T(2,128)} %param.11) | copy-start | bytes 3076
  6.5 123.1 %all-gather.5.cloned.1.call-start = ((), (), s32[]{:S(2)}) async-start(), calls=%async_computation.3 | async-start | bytes 14796800 | tf_op jit(solution)/shard_map/all_gather | solution.py:46
  9.9 127.5 %all-to-all-start = ((bf16[8,400,384]{2,1,0:T(8,128)(2,1)}), bf16[8,400,384]{2,1,0:T(8,128)(2,1)S(1)}, u32[]{:S(2)}, u32[]{:S(2)}) async-start(bf16[8,400,384]{2,1,0:T(8,128)(2,1)} %stack.4), calls=%async_computation | async-start | bytes 4915200 | tf_op jit(solution)/shard_map/all_to_all | solution.py:57
  16.0 298.3 %all-gather.7.cloned.1.call-start = ((), (), s32[]{:S(2)}) async-start(), calls=%async_computation.4 | async-start | bytes 9469952 | tf_op jit(solution)/shard_map/all_gather | solution.py:102
  16.1 121.3 %copy-start.5 = (f32[3200]{0:T(1024)S(1)}, f32[3200]{0:T(1024)}, u32[]{:S(2)}) copy-start(f32[3200]{0:T(1024)} %param.9) | copy-start | bytes 38404
  211.5 3.4 copy-start
  214.9 5.9 %copy-start.1 = (bf16[128,400]{0,1:T(8,128)(2,1)S(1)}, bf16[128,400]{0,1:T(8,128)(2,1)}, u32[]{:S(2)}) copy-start(bf16[128,400]{0,1:T(8,128)(2,1)} %param.12) | copy-start | bytes 307204
  214.9 49.3 %copy-start.3 = (s32[8,2]{0,1:T(2,128)S(1)}, s32[8,2]{0,1:T(2,128)}, u32[]{:S(2)}) copy-start(s32[8,2]{0,1:T(2,128)} %param.15) | copy-start | bytes 196
  214.9 49.3 %copy-start.4 = (s32[8,2]{0,1:T(2,128)S(1)}, s32[8,2]{0,1:T(2,128)}, u32[]{:S(2)}) copy-start(s32[8,2]{0,1:T(2,128)} %param.14) | copy-start | bytes 196
  250.7 32.1 %all-to-all-start.1 = ((bf16[128,16,200]{0,2,1:T(8,128)(2,1)}), bf16[128,16,200]{0,2,1:T(8,128)(2,1)S(1)}, u32[]{:S(2)}, u32[]{:S(2)}) async-start(bf16[128,16,200]{0,2,1:T(8,128)(2,1)} %bitcast.13), calls=%async_computation.1 | async-start | bytes 1638400 | tf_op jit(solution)/shard_map/all_to_all | solution.py:101
  357.6 95.9 %all-to-all-start.2 = ((bf16[8,2,256,800]{2,3,1,0:T(8,128)(2,1)}), bf16[8,2,256,800]{2,3,1,0:T(8,128)(2,1)}, u32[]{:S(2)}, u32[]{:S(2)}) async-start(bf16[8,2,256,800]{2,3,1,0:T(8,128)(2,1)} %broadcast_select_fusion), calls=%async_computation.2 | async-start | bytes 13107200 | tf_op jit(solution)/shard_map/all_to_all | solution.py:120
Sparse Core Ops, SparseCore 0:
  9.8 119.8 all-gather.4
  220.9 93.3 all-gather.6
